TPU v7x, 128 devices: a whole 4x4x4 slice. The times are simulated.
128 devices in a mesh: blk: 32 (over x, z_hi, y), rep: 4 (over z_lo, core).
Axes of the slice: x: 4, y: 4, z: 4 (z_hi: 2, z_lo: 2; z = z_hi * 2 + z_lo), core: 2. Of those that a mesh axis runs over, the one named last changes fastest.
Arguments:
- queries: bfloat16 [32768, 4096], P(('blk', 'rep')), as said below
- query_group: int32 [32768, 1], P(('blk', 'rep')), may hold values from 0 to 3; in each aligned block of 256 rows (0 to 255, 256 to 511, ...) at most 128 rows name the same one
- query_bin: int32 [32768], P(('blk', 'rep')), may hold values from 0 to 63
- query_shift: int32 [32768], P(('blk', 'rep')), may hold values from 1 to 2
- library: bfloat16 [4, 1024, 4096], P('rep', 'blk'), as said below
- library_bin: int32 [4, 1024], P('rep', 'blk'), may hold values from 0 to 63
Outputs:
- best_scores: float32 [32768, 8], P(('blk', 'rep'))
Inputs may be any that keep to these rules, and one draw needn't show every extreme that they name: `query_group`: among the 256 queries of one device at most 128 name the same group, and on every draw some device has a group named by exactly 128 of its queries. `queries`: intensities are nonnegative and every spectrum has peaks. `library`: intensities are nonnegative and every spectrum has peaks.
All inputs are finite; a program needn't handle non-finite values.
Results may differ from a plain program's by a relative error of at most 0.0021.
Values may be sent and summed in bfloat16 or wider, within the bound.
No kernel may reach another device: no remote copies, remote signals or barrier semaphores. Data moves between devices by JAX's collectives and lax.ppermute only.
A program may use at most 192 MiB of HBM per device.

v0:
```python
import jax
import jax.numpy as jnp
from jax import lax
from jax.sharding import Mesh
from jax.sharding import PartitionSpec as P

W = 4096
K = 8
NSHIFT = 2
SHIFT_BINS = 16
WIN = 16
CAP = 128
BLK = ("blk_0", "blk_1", "blk_2")
BLK_REP = ("blk_0", "blk_1", "blk_2", "rep")
ZRING = ("blk_1", "rep")


def ring_index(z, core):
    return z // 2 * 4 + z % 2 * 2 + core


UP = [(ring_index(z, 0), ring_index((z + 1) % 4, 0)) for z in range(4)] + [
    (ring_index(z, 1), ring_index((z + 3) % 4, 1)) for z in range(4)
]
CROSS = [(ring_index(z, 1), ring_index((z + 1) % 4, 0)) for z in range(4)] + [
    (ring_index(z, 0), ring_index((z + 3) % 4, 1)) for z in range(4)
]
SIBLING = [(ring_index(z, c), ring_index(z, 1 - c)) for z in range(4) for c in range(2)]


def inverse(perm):
    return [(b, a) for a, b in perm]


def unit_rows(raw):
    values = jnp.sqrt(raw.astype(jnp.float32))
    total = jnp.sum(values * values, axis=-1, keepdims=True)
    return (values * lax.rsqrt(total + 1e-06)).astype(jnp.bfloat16)


def lower_bins(rows, amount):
    tail = jnp.zeros(rows.shape[:-1] + (amount,), rows.dtype)
    return jnp.concatenate([rows[..., amount:], tail], axis=-1)


def slot_index(role, roles, capacity):
    labels = jnp.arange(roles, dtype=jnp.int32)
    onehot = (role[:, None] == labels[None, :]).astype(jnp.int32)
    before = jnp.cumsum(onehot, axis=0) - onehot
    place = jnp.sum(before * onehot, axis=1)
    return role * capacity + place


def top_rows(scores):
    height = scores.shape[0]
    position = lax.broadcasted_iota(jnp.int32, scores.shape, 0)
    picked = []
    for step in range(K):
        top = jnp.max(scores, axis=0)
        first = jnp.min(jnp.where(scores == top[None, :], position, height), axis=0)
        picked.append(top)
        scores = jnp.where(position == first[None, :], -3e38, scores)
    return jnp.stack(picked, axis=1)


def route(blocks, perms):
    return [blocks[0]] + [lax.ppermute(b, ZRING, p) for b, p in zip(blocks[1:], perms)]


def on_device(queries, query_group, query_bin, query_shift, library, library_bin):
    lib_rows = library.shape[1]
    z_lo = lax.axis_index("rep") // 2
    core = lax.axis_index("rep") % 2
    roles = 4
    slots = roles * CAP
    unit_lib = unit_rows(library[0])
    bin_row = jnp.pad(library_bin.astype(jnp.bfloat16), ((0, 0), (0, W - lib_rows)))
    packed_lib = jnp.concatenate([unit_lib, bin_row], axis=0)
    half = lax.all_gather(packed_lib, "blk_1", axis=0, tiled=True)
    full = lax.all_gather(half, ("blk_0", "blk_2"), axis=0, tiled=True)
    stride = lib_rows + 1
    blocks_n = full.shape[0] // stride
    lib_bins = full.reshape(blocks_n, stride, W)[:, lib_rows, :stride].reshape(-1)
    lib_bins = lib_bins.astype(jnp.int32)
    valid = jnp.arange(full.shape[0], dtype=jnp.int32) % stride != lib_rows
    unit_q = unit_rows(queries)
    group = query_group[:, 0]
    role = (group // 2 != z_lo).astype(jnp.int32) * 2 + (group % 2 != core).astype(jnp.int32)
    slot = slot_index(role, roles, CAP)
    slot_ids = jnp.arange(slots, dtype=jnp.int32)
    placed = slot[:, None] == slot_ids[None, :]
    placed_int = placed.astype(jnp.int32)
    send_q = (
        lax.dot_general(
            placed.astype(jnp.bfloat16),
            unit_q,
            (((0,), (0,)), ((), ())),
            preferred_element_type=jnp.float32,
        )
        .astype(jnp.bfloat16)
        .reshape(roles, CAP, W)
    )
    send_bin = jnp.sum(placed_int * query_bin[:, None], axis=0).reshape(roles, CAP)
    send_shift = jnp.sum(placed_int * query_shift[:, None], axis=0).reshape(roles, CAP)
    send_meta = jnp.stack([send_bin, send_shift], axis=1)
    perms = (SIBLING, UP, CROSS)
    rows = jnp.concatenate(route([send_q[i] for i in range(roles)], perms), axis=0)
    meta = jnp.stack(route([send_meta[i] for i in range(roles)], perms), axis=0)
    flat_bin = meta[:, 0].reshape(-1)
    flat_shift = meta[:, 1].reshape(-1)
    total = rows.shape[0]
    moved = jnp.zeros_like(rows)
    for s in range(1, NSHIFT + 1):
        moved = jnp.where((flat_shift == s)[:, None], lower_bins(rows, s * SHIFT_BINS), moved)
    both = jnp.concatenate([rows, moved], axis=0)
    prod = lax.dot_general(full, both, (((1,), (1,)), ((), ())), preferred_element_type=jnp.float32)
    near = (jnp.abs(lib_bins[:, None] - flat_bin[None, :]) <= WIN) & valid[:, None]
    scores = jnp.where(near, jnp.maximum(prod[:, :total], prod[:, total:]), 0.0)
    scores = jnp.where(valid[:, None], scores, -1.0)
    best = top_rows(scores).reshape(roles, CAP, K)
    home = route([best[i] for i in range(roles)], tuple((inverse(p) for p in perms)))
    home = jnp.concatenate(home, axis=0)
    return jnp.take(home, slot, axis=0)


def solution(mesh):
    split = Mesh(
        mesh.devices.reshape(4, 2, 4, mesh.shape["rep"]), ("blk_0", "blk_1", "blk_2", "rep")
    )
    in_specs = (
        P(BLK_REP, None),
        P(BLK_REP, None),
        P(BLK_REP),
        P(BLK_REP),
        P("rep", BLK, None),
        P("rep", BLK),
    )
    out_specs = P(BLK_REP, None)
    return jax.shard_map(
        on_device, mesh=split, in_specs=in_specs, out_specs=out_specs, check_vma=False
    )
```

profile of v0, /device:TPU:0, one launch (start us, length us, event | category | flops | bytes accessed | tf_op | source)
XLA Modules:
  0.0 165.7 jit_solution(16801492224332433308)
XLA Ops:
  6.5 1.4 fusion.15
  7.9 1.1 fusion.16
  9.1 0.7 convert_element_type.53
  9.7 12.3 %all-gather = bf16[2,33,4096]{2,1,0:T(8,128)(2,1)S(1)} all-gather(bf16[1,33,4096]{2,1,0:T(8,128)(2,1)S(1)} %fusion.18), channel_id=1, replica_groups=mesh['blk_0'=4,'blk_1'=2,'blk_2'=4,'rep'=4] {'blk_1'}, dimensions={0}, use_global_device_ids=true | all-gather | bytes 811008 | tf_op jit(solution)/shard_map/all_gather | solution.py:79
  22.1 0.9 reshape.119
  23.0 0.0 all-gather.4.cloned.1.call-update
  23.1 1.2 reduce-window.6
  24.3 0.1 slice.94
  24.4 0.1 copy.31
  24.6 0.1 copy.32
  24.6 0.1 add_bitcast_fusion
  24.8 1.4 multiply_reduce_fusion
  26.2 2.0 %convolution_convert_fusion = bf16[512,4096]{1,0:T(8,128)(2,1)S(1)} fusion(bf16[256,4096]{1,0:T(8,128)(2,1)S(1)} %copy-done, f32[256]{0:T(256)S(1)} %add_rsqrt_fusion, s32[256]{0:T(256)S(1)} %bitcast.72), kind=kOutput, calls=%fused_computation.1 | convolution fusion | flops 1079115776 | bytes 6293504 | tf_op jit(solution)/shard_map/dot_general | solution.py:94
  28.2 0.0 copy-start.2
  28.2 0.0 copy-start.3
  28.2 1.7 %fusion.39 = (bf16[128,4096]{1,0:T(8,128)(2,1)S(1)}, bf16[1024,4096]{1,0:T(8,128)(2,1)}, bf16[128,4096]{1,0:T(8,128)(2,1)S(1)}, bf16[128,4096]{1,0:T(8,128)(2,1)S(1)}, bf16[128,4096]{1,0:T(8,128)(2,1)S(1)}) fusion(bf16[512,4096]{1,0:T(8,128)(2,1)S(1)} %convolution_convert_fusion), kind=kLoop, calls=%fused_computation.106 | loop fusion | bytes 9437184 | tf_op jit(solution)/shard_map/slice | solution.py:107
  29.9 0.0 collective-permute-start.3
  29.9 1.3 collective-permute-start.4
  31.2 2.3 %collective-permute-start.5 = (bf16[128,4096]{1,0:T(8,128)(2,1)S(1)}, bf16[128,4096]{1,0:T(8,128)(2,1)S(1)}, u32[]{:S(2)}, u32[]{:S(2)}) collective-permute-start(bf16[128,4096]{1,0:T(8,128)(2,1)S(1)} %get-tuple-element.14), channel_id=1, source_target_pairs={{1,2},{3,16},{17,18},{19,0},{0,19},{2,1},{16,3},{18,17},{5,6},{7,2... | collective-permute-start | bytes 3145736 | tf_op jit(solution)/shard_map/ppermute | solution.py:67
  33.6 0.2 select_reduce_fusion.9
  33.8 0.1 collective-permute-start
  33.9 1.7 %collective-permute-start.1 = (s32[2,128]{1,0:T(2,128)S(1)}, s32[2,128]{1,0:T(2,128)S(1)}, u32[]{:S(2)}, u32[]{:S(2)}) collective-permute-start(s32[2,128]{1,0:T(2,128)S(1)} %get-tuple-element.26), channel_id=1, source_target_pairs={{0,2},{2,16},{16,18},{18,0},{1,19},{3,1},{17,3},{19,17},{4,6},{6,2... | collective-permute-start | bytes 3080 | tf_op jit(solution)/shard_map/ppermute | solution.py:67
  35.5 0.2 collective-permute-start.2
  35.7 21.2 %collective-permute-done.1 = s32[2,128]{1,0:T(2,128)S(1)} collective-permute-done((s32[2,128]{1,0:T(2,128)S(1)}, s32[2,128]{1,0:T(2,128)S(1)}, u32[]{:S(2)}, u32[]{:S(2)}) %collective-permute-start.1) | collective-permute-done | bytes 1056 | tf_op jit(solution)/shard_map/ppermute | solution.py:67
  56.9 0.5 collective-permute-done.2
  57.4 0.0 collective-permute-done.4
  57.5 0.5 pad_maximum_fusion
  58.0 3.2 %slice.108 = bf16[512,4064]{1,0:T(8,128)(2,1)S(1)} slice(bf16[512,4096]{1,0:T(8,128)(2,1)S(1)} %pad_maximum_fusion), slice={[0:512], [32:4096]} | slice | bytes 8323072 | tf_op jit(solution)/shard_map/slice | solution.py:43
  61.2 3.2 %slice.109 = bf16[512,4080]{1,0:T(8,128)(2,1)S(1)} slice(bf16[512,4096]{1,0:T(8,128)(2,1)S(1)} %pad_maximum_fusion), slice={[0:512], [16:4096]} | slice | bytes 8355840 | tf_op jit(solution)/shard_map/slice | solution.py:43
  64.4 1.1 constant_dynamic-update-slice_fusion.2
  65.5 1.1 constant_dynamic-update-slice_fusion.1
  66.5 1.1 constant_dynamic-update-slice_fusion
  67.6 4.1 %select_dynamic-update-slice_fusion = bf16[1024,4096]{1,0:T(8,128)(2,1)} fusion(bf16[1024,4096]{1,0:T(8,128)(2,1)} %constant_dynamic-update-slice_fusion, bf16[512,4080]{1,0:T(8,128)(2,1)S(1)} %slice.109, bf16[512,4064]{1,0:T(8,128)(2,1)S(1)} %slice.108, pred[512]{0:T(512)(128)(4,1)S(1)} %get-tuple-element.22, pred[512]{0:T(512)(128)(4,1)S(1)} %get-tuple-element.21), kind=kLoop, calls=%fused_computation.3 | loop fusion | flops 4194304 | bytes 12534784 | tf_op jit(solution)/shard_map/concatenate | solution.py:115
  71.8 28.8 %all-gather.4.cloned.1.call-done = bf16[16,66,4096]{2,1,0:T(8,128)(2,1)} async-done(((bf16[1,66,4096]{2,1,0:T(8,128)(2,1)}), bf16[16,66,4096]{2,1,0:T(8,128)(2,1)}) %all-gather.4.cloned.1.call-update) | async-done | bytes 8650768 | tf_op jit(solution)/shard_map/all_gather | solution.py:80
  100.6 13.2 %reshape.107 = bf16[32,33,4096]{2,1,0:T(8,128)(2,1)} reshape(bf16[16,66,4096]{2,1,0:T(8,128)(2,1)} %all-gather.4.cloned.1.call-done) | data formatting | bytes 17301504 | tf_op jit(solution)/shard_map/reshape | solution.py:83
  113.7 0.9 fusion.21
  114.6 0.1 reshape.108
  114.7 8.2 %reshape.120 = bf16[1056,4096]{1,0:T(8,128)(2,1)} reshape(bf16[16,66,4096]{2,1,0:T(8,128)(2,1)} %all-gather.4.cloned.1.call-done) | data formatting | bytes 17301504
  122.9 13.0 %fusion.41 = f32[1056,1024]{1,0:T(8,128)S(1)} fusion(bf16[1056,4096]{1,0:T(8,128)(2,1)} %reshape.120, bf16[1024,4096]{1,0:T(8,128)(2,1)} %select_dynamic-update-slice_fusion), kind=kOutput, calls=%fused_computation.108 | convolution fusion | flops 8858370048 | bytes 21364736 | tf_op jit(solution)/shard_map/dot_general | solution.py:116
  135.9 1.4 fusion.37
  137.3 0.4 select_reduce_fusion.7
  137.7 0.4 fusion.13
  138.0 0.5 select_reduce_fusion.6
  138.6 0.5 fusion.12
  139.1 0.8 select_reduce_fusion.5
  139.8 0.7 fusion.36
  140.5 0.9 select_reduce_fusion.4
  141.4 0.8 fusion.11
  142.3 1.1 select_reduce_fusion.3
  143.4 1.0 fusion.20
  144.5 1.3 select_reduce_fusion.2
  145.7 1.2 fusion.10
  147.0 1.5 select_reduce_fusion.1
  148.4 1.4 select_reduce_fusion
  149.8 0.1 collective-permute-start.6
  149.9 3.0 %collective-permute-start.7 = (f32[128,8]{0,1:T(8,128)S(1)}, f32[128,8]{0,1:T(8,128)S(1)}, u32[]{:S(2)}, u32[]{:S(2)}) collective-permute-start(f32[128,8]{0,1:T(8,128)S(1)} %get-tuple-element.19), channel_id=1, source_target_pairs={{2,0},{16,2},{18,16},{0,18},{19,1},{1,3},{3,17},{17,19},{6,4},{20,... | collective-permute-start | bytes 12296 | tf_op jit(solution)/shard_map/ppermute | solution.py:67
  153.0 0.0 collective-permute-start.8
  153.0 0.0 collective-permute-done.6
  153.0 1.3 collective-permute-done.7
  154.3 2.9 %collective-permute-done.8 = f32[128,8]{0,1:T(8,128)S(1)} collective-permute-done((f32[128,8]{0,1:T(8,128)S(1)}, f32[128,8]{0,1:T(8,128)S(1)}, u32[]{:S(2)}, u32[]{:S(2)}) %collective-permute-start.8) | collective-permute-done | bytes 4128 | tf_op jit(solution)/shard_map/ppermute | solution.py:67
  157.2 0.1 copy.36
  157.3 0.7 gather_fusion
  158.1 0.1 broadcast_select_fusion
  158.2 0.7 copy.37
  (28 shorter events, 0.3 us)
Async XLA Ops:
  6.5 16.5 %copy-start.1 = (s32[256,1]{0,1:T(1,128)S(1)}, s32[256,1]{0,1:T(1,128)}, u32[]{:S(2)}) copy-start(s32[256,1]{0,1:T(1,128)} %param.7) | copy-start | bytes 3076
  6.5 18.2 %copy-start = (bf16[256,4096]{1,0:T(8,128)(2,1)S(1)}, bf16[256,4096]{1,0:T(8,128)(2,1)}, u32[]{:S(2)}) copy-start(bf16[256,4096]{1,0:T(8,128)(2,1)} %param.6) | copy-start | bytes 6291460
  6.5 94.0 %all-gather.4.cloned.1.call-start = ((), (), s32[]{:S(2)}) async-start(), calls=%async_computation | async-start | bytes 10027008 | tf_op jit(solution)/shard_map/all_gather | solution.py:80
  28.2 5.4 %copy-start.2 = (s32[256]{0:T(256)S(1)}, s32[256]{0:T(256)}, u32[]{:S(2)}) copy-start(s32[256]{0:T(256)} %param.8) | copy-start | bytes 3076
  28.2 5.3 %copy-start.3 = (s32[256]{0:T(256)S(1)}, s32[256]{0:T(256)}, u32[]{:S(2)}) copy-start(s32[256]{0:T(256)} %param.9) | copy-start | bytes 3076
  29.9 27.5 %collective-permute-start.3 = (bf16[128,4096]{1,0:T(8,128)(2,1)S(1)}, bf16[128,4096]{1,0:T(8,128)(2,1)S(1)}, u32[]{:S(2)}, u32[]{:S(2)}) collective-permute-start(bf16[128,4096]{1,0:T(8,128)(2,1)S(1)} %get-tuple-element.16), channel_id=1, source_target_pairs={{0,1},{1,0},{2,3},{3,2},{16,17},{17,16},{18,19},{19,18},{4,5},{5,4... | collective-permute-start | bytes 3145736 | tf_op jit(solution)/shard_map/ppermute | solution.py:67
  29.9 27.5 %collective-permute-start.4 = (bf16[128,4096]{1,0:T(8,128)(2,1)S(1)}, bf16[128,4096]{1,0:T(8,128)(2,1)S(1)}, u32[]{:S(2)}, u32[]{:S(2)}) collective-permute-start(bf16[128,4096]{1,0:T(8,128)(2,1)S(1)} %get-tuple-element.15), channel_id=1, source_target_pairs={{0,2},{2,16},{16,18},{18,0},{1,19},{3,1},{17,3},{19,17},{4,6},{6,2... | collective-permute-start | bytes 3145736 | tf_op jit(solution)/shard_map/ppermute | solution.py:67
  31.2 26.2 %collective-permute-start.5 = (bf16[128,4096]{1,0:T(8,128)(2,1)S(1)}, bf16[128,4096]{1,0:T(8,128)(2,1)S(1)}, u32[]{:S(2)}, u32[]{:S(2)}) collective-permute-start(bf16[128,4096]{1,0:T(8,128)(2,1)S(1)} %get-tuple-element.14), channel_id=1, source_target_pairs={{1,2},{3,16},{17,18},{19,0},{0,19},{2,1},{16,3},{18,17},{5,6},{7,2... | collective-permute-start | bytes 3145736 | tf_op jit(solution)/shard_map/ppermute | solution.py:67
  33.8 1.8 %collective-permute-start = (s32[2,128]{1,0:T(2,128)S(1)}, s32[2,128]{1,0:T(2,128)S(1)}, u32[]{:S(2)}, u32[]{:S(2)}) collective-permute-start(s32[2,128]{1,0:T(2,128)S(1)} %get-tuple-element.24), channel_id=1, source_target_pairs={{0,1},{1,0},{2,3},{3,2},{16,17},{17,16},{18,19},{19,18},{4,5},{5,4... | collective-permute-start | bytes 3080 | tf_op jit(solution)/shard_map/ppermute | solution.py:67
  33.9 23.0 %collective-permute-start.1 = (s32[2,128]{1,0:T(2,128)S(1)}, s32[2,128]{1,0:T(2,128)S(1)}, u32[]{:S(2)}, u32[]{:S(2)}) collective-permute-start(s32[2,128]{1,0:T(2,128)S(1)} %get-tuple-element.26), channel_id=1, source_target_pairs={{0,2},{2,16},{16,18},{18,0},{1,19},{3,1},{17,3},{19,17},{4,6},{6,2... | collective-permute-start | bytes 3080 | tf_op jit(solution)/shard_map/ppermute | solution.py:67
  35.5 21.8 %collective-permute-start.2 = (s32[2,128]{1,0:T(2,128)S(1)}, s32[2,128]{1,0:T(2,128)S(1)}, u32[]{:S(2)}, u32[]{:S(2)}) collective-permute-start(s32[2,128]{1,0:T(2,128)S(1)} %get-tuple-element.25), channel_id=1, source_target_pairs={{1,2},{3,16},{17,18},{19,0},{0,19},{2,1},{16,3},{18,17},{5,6},{7,2... | collective-permute-start | bytes 3080 | tf_op jit(solution)/shard_map/ppermute | solution.py:67
  149.8 3.2 %collective-permute-start.6 = (f32[128,8]{0,1:T(8,128)S(1)}, f32[128,8]{0,1:T(8,128)S(1)}, u32[]{:S(2)}, u32[]{:S(2)}) collective-permute-start(f32[128,8]{0,1:T(8,128)S(1)} %get-tuple-element.20), channel_id=1, source_target_pairs={{1,0},{0,1},{3,2},{2,3},{17,16},{16,17},{19,18},{18,19},{5,4},{4,5... | collective-permute-start | bytes 12296 | tf_op jit(solution)/shard_map/ppermute | solution.py:67
  149.9 4.3 %collective-permute-start.7 = (f32[128,8]{0,1:T(8,128)S(1)}, f32[128,8]{0,1:T(8,128)S(1)}, u32[]{:S(2)}, u32[]{:S(2)}) collective-permute-start(f32[128,8]{0,1:T(8,128)S(1)} %get-tuple-element.19), channel_id=1, source_target_pairs={{2,0},{16,2},{18,16},{0,18},{19,1},{1,3},{3,17},{17,19},{6,4},{20,... | collective-permute-start | bytes 12296 | tf_op jit(solution)/shard_map/ppermute | solution.py:67
  153.0 4.2 %collective-permute-start.8 = (f32[128,8]{0,1:T(8,128)S(1)}, f32[128,8]{0,1:T(8,128)S(1)}, u32[]{:S(2)}, u32[]{:S(2)}) collective-permute-start(f32[128,8]{0,1:T(8,128)S(1)} %get-tuple-element.18), channel_id=1, source_target_pairs={{2,1},{16,3},{18,17},{0,19},{19,0},{1,2},{3,16},{17,18},{6,5},{20,... | collective-permute-start | bytes 12296 | tf_op jit(solution)/shard_map/ppermute | solution.py:67
Sparse Core Ops, SparseCore 0:
  23.2 77.3 all-gather.3
where the time goes:
time: 166 us
  waiting for transfers between devices  54.7 us (33%)
  local copies, waits for them, and re-layouts  35.5 us (21%)
  other arithmetic  25.8 us (16%)
  matrix products  15 us (9%)
  between operations  13.6 us (8%)
  blocking collectives  12.3 us (7%)
  starting transfers between devices  8.72 us (5%)
    all_gather x1, waiting for transfers between devices, on_device(): full = lax.all_gather(half, ('blk_0', 'blk_2'), axis=0, tiled=True)  28.8 us
    ppermute x9, waiting for transfers between devices, route(): lax.ppermute(b, ZRING, p)  25.9 us
    reshape x1, local copies, waits for them, and re-layouts, on_device(): full.reshape(blocks_n, stride, W)[:, lib_rows, :stride].reshape(-1)  13.2 us
    dot_general x1, matrix products, on_device(): lax.dot_general(full, both, (((1,), (1,)), ((), ())), preferred_element_t...  13 us
    all_gather x1, blocking collectives, on_device(): half = lax.all_gather(packed_lib, 'blk_1', axis=0, tiled=True)  12.3 us
    unnamed x13, local copies, waits for them, and re-layouts  12.3 us
    ppermute x9, starting transfers between devices, route(): lax.ppermute(b, ZRING, p)  8.72 us
    reduce_max x8, other arithmetic, top_rows(): top = jnp.max(scores, axis=0)  7.39 us
  transfers between devices with their start and end apart: 10, of which 5 were waited for; matrix products, arithmetic and copies ran while one was open for 13% of the time, Pallas kernels for 0%

commit v1 on v0

--- a/solution.py
+++ b/solution.py
@@ -77,7 +77,12 @@
     bin_row = jnp.pad(library_bin.astype(jnp.bfloat16), ((0, 0), (0, W - lib_rows)))
     packed_lib = jnp.concatenate([unit_lib, bin_row], axis=0)
     half = lax.all_gather(packed_lib, "blk_1", axis=0, tiled=True)
-    full = lax.all_gather(half, ("blk_0", "blk_2"), axis=0, tiled=True)
+    full = jnp.concatenate(
+        lax.all_to_all(
+            jnp.stack([half] * lax.axis_size(("blk_0", "blk_2"))), ("blk_0", "blk_2"), 0, 0
+        ),
+        axis=0,
+    )
     stride = lib_rows + 1
     blocks_n = full.shape[0] // stride
     lib_bins = full.reshape(blocks_n, stride, W)[:, lib_rows, :stride].reshape(-1)

time: 166 us -> 248 us (1.49); the launches traced: 166 us -> 245 us
  waiting for transfers between devices: 54.7 us -> 136 us
  between operations: 13.6 us -> 0.27 us
  starting transfers between devices: 8.72 us -> 16 us
  local copies, waits for them, and re-layouts: 35.5 us -> 39.5 us
    all_to_all x0 -> x1, waiting for transfers between devices: none -> 113 us  [on_device(): lax.all_to_all(jnp.stack([half] * lax.axis_size(('blk_0', 'blk_2'))), ('b...]
    all_gather x1 -> x0, waiting for transfers between devices: 28.8 us -> none  [on_device(): full = lax.all_gather(half, ('blk_0', 'blk_2'), axis=0, tiled=True)]
    another operation x2 -> x4, local copies, waits for them, and re-layouts: 0.1 us -> 18.1 us  [the longest x1 13.2 us: on_device(): full.reshape(blocks_n, stride, W)[:, lib_rows, :stride].reshape(-1)]
    unnamed x13 -> x12, local copies, waits for them, and re-layouts: 12.3 us -> 3.37 us
    all_to_all x0 -> x1, starting transfers between devices: none -> 7.21 us  [on_device(): lax.all_to_all(jnp.stack([half] * lax.axis_size(('blk_0', 'blk_2'))), ('b...]
    reshape x1, local copies, waits for them, and re-layouts: 13.2 us -> 8.16 us  [on_device(): jnp.concatenate(lax.all_to_all(jnp.stack([half] * lax.axis_size(('blk_0',...]
    ppermute x9, waiting for transfers between devices: 25.9 us -> 23 us  [route(): lax.ppermute(b, ZRING, p)]
  transfers between devices with their start and end apart: 10 -> 10, of which waited for: 5 -> 5; matrix products, arithmetic and copies ran while one was open for 13% -> 9% of each run, Pallas kernels for 0% -> 0%
where the time goes in v1:
time: 248 us; the launch traced here: 245 us
  waiting for transfers between devices  136 us (55%)
  local copies, waits for them, and re-layouts  39.5 us (16%)
  other arithmetic  25.7 us (10%)
  starting transfers between devices  16 us (6%)
  matrix products  14.9 us (6%)
  blocking collectives  12.3 us (5%)
    all_to_all x1, waiting for transfers between devices, on_device(): lax.all_to_all(jnp.stack([half] * lax.axis_size(('blk_0', 'blk_2'))), ('b...  113 us
    ppermute x9, waiting for transfers between devices, route(): lax.ppermute(b, ZRING, p)  23 us
    another operation x1, local copies, waits for them, and re-layouts, on_device(): full.reshape(blocks_n, stride, W)[:, lib_rows, :stride].reshape(-1)  13.2 us
    dot_general x1, matrix products, on_device(): lax.dot_general(full, both, (((1,), (1,)), ((), ())), preferred_element_t...  13 us
    all_gather x1, blocking collectives, on_device(): half = lax.all_gather(packed_lib, 'blk_1', axis=0, tiled=True)  12.3 us
    ppermute x9, starting transfers between devices, route(): lax.ppermute(b, ZRING, p)  8.76 us
    reshape x1, local copies, waits for them, and re-layouts, on_device(): jnp.concatenate(lax.all_to_all(jnp.stack([half] * lax.axis_size(('blk_0',...  8.16 us
    reduce_max x8, other arithmetic, top_rows(): top = jnp.max(scores, axis=0)  7.39 us
  transfers between devices with their start and end apart: 10, of which 5 were waited for; matrix products, arithmetic and copies ran while one was open for 9% of the time, Pallas kernels for 0%

profile of v1, /device:TPU:0, one launch (start us, length us, event | category | flops | bytes accessed | tf_op | source)
XLA Modules:
  0.0 245.0 jit_solution(3776104924431081186)
XLA Ops:
  0.0 1.2 fusion.15
  1.2 1.1 fusion.16
  2.4 0.7 convert_element_type.53
  3.1 12.3 %all-gather = bf16[2,33,4096]{2,1,0:T(8,128)(2,1)S(1)} all-gather(bf16[1,33,4096]{2,1,0:T(8,128)(2,1)S(1)} %fusion.18), channel_id=1, replica_groups=mesh['blk_0'=4,'blk_1'=2,'blk_2'=4,'rep'=4] {'blk_1'}, dimensions={0}, use_global_device_ids=true | all-gather | bytes 811008 | tf_op jit(solution)/shard_map/all_gather | solution.py:79
  15.4 0.1 reshape.120
  15.5 4.8 %stack.30 = bf16[16,66,4096]{2,1,0:T(8,128)(2,1)} broadcast(bf16[66,4096]{1,0:T(8,128)(2,1)S(1)} %reshape.120), dimensions={1,2} | broadcast | bytes 9191424 | tf_op jit(solution)/shard_map/stack | solution.py:82
  20.3 7.2 %all-to-all-start = ((bf16[16,66,4096]{2,1,0:T(8,128)(2,1)}), bf16[16,66,4096]{2,1,0:T(8,128)(2,1)}, u32[]{:S(2)}, u32[]{:S(2)}) async-start(bf16[16,66,4096]{2,1,0:T(8,128)(2,1)} %stack.30), calls=%async_computation | async-start | bytes 18874368 | tf_op jit(solution)/shard_map/all_to_all | solution.py:81
  27.6 1.2 reduce-window.6
  28.8 0.1 slice.94
  28.9 0.1 copy.31
  29.1 0.1 copy.32
  29.2 0.1 add_bitcast_fusion
  29.3 1.4 multiply_reduce_fusion
  30.7 2.0 convolution_convert_fusion
  32.7 0.0 copy-start.2
  32.7 0.0 copy-start.3
  32.7 1.7 fusion.39
  34.4 1.3 collective-permute-start.4
  35.7 2.4 collective-permute-start.5
  38.1 0.2 select_reduce_fusion.9
  38.3 0.1 collective-permute-start
  38.4 1.7 collective-permute-start.1
  40.1 0.0 collective-permute-done
  40.1 0.2 collective-permute-start.2
  40.3 21.2 %collective-permute-done.1 = s32[2,128]{1,0:T(2,128)S(1)} collective-permute-done((s32[2,128]{1,0:T(2,128)S(1)}, s32[2,128]{1,0:T(2,128)S(1)}, u32[]{:S(2)}, u32[]{:S(2)}) %collective-permute-start.1) | collective-permute-done | bytes 1056 | tf_op jit(solution)/shard_map/ppermute | solution.py:67
  61.4 0.5 collective-permute-done.2
  62.0 0.0 collective-permute-done.3
  62.0 0.5 pad_maximum_fusion
  62.5 3.2 %slice.108 = bf16[512,4064]{1,0:T(8,128)(2,1)S(1)} slice(bf16[512,4096]{1,0:T(8,128)(2,1)S(1)} %pad_maximum_fusion), slice={[0:512], [32:4096]} | slice | bytes 8323072 | tf_op jit(solution)/shard_map/slice | solution.py:43
  65.7 3.2 %slice.109 = bf16[512,4080]{1,0:T(8,128)(2,1)S(1)} slice(bf16[512,4096]{1,0:T(8,128)(2,1)S(1)} %pad_maximum_fusion), slice={[0:512], [16:4096]} | slice | bytes 8355840 | tf_op jit(solution)/shard_map/slice | solution.py:43
  68.9 1.1 constant_dynamic-update-slice_fusion.2
  70.0 1.1 constant_dynamic-update-slice_fusion.1
  71.1 1.1 constant_dynamic-update-slice_fusion
  72.2 4.1 %select_dynamic-update-slice_fusion = bf16[1024,4096]{1,0:T(8,128)(2,1)} fusion(bf16[1024,4096]{1,0:T(8,128)(2,1)} %constant_dynamic-update-slice_fusion, bf16[512,4080]{1,0:T(8,128)(2,1)S(1)} %slice.109, bf16[512,4064]{1,0:T(8,128)(2,1)S(1)} %slice.108, pred[512]{0:T(512)(128)(4,1)S(1)} %get-tuple-element.22, pred[512]{0:T(512)(128)(4,1)S(1)} %get-tuple-element.21), kind=kLoop, calls=%fused_computation.3 | loop fusion | flops 4194304 | bytes 12534784 | tf_op jit(solution)/shard_map/concatenate | solution.py:120
  76.3 113.3 %all-to-all-done = bf16[16,66,4096]{2,1,0:T(8,128)(2,1)} async-done(((bf16[16,66,4096]{2,1,0:T(8,128)(2,1)}), bf16[16,66,4096]{2,1,0:T(8,128)(2,1)}, u32[]{:S(2)}, u32[]{:S(2)}) %all-to-all-start) | async-done | bytes 8650784 | tf_op jit(solution)/shard_map/all_to_all | solution.py:81
  189.6 13.2 %reshape_reshape.3 = bf16[32,33,4096]{2,1,0:T(8,128)(2,1)} reshape(bf16[16,66,4096]{2,1,0:T(8,128)(2,1)} %all-to-all-done) | data formatting | bytes 17301504 | tf_op jit(solution)/shard_map/reshape;reshape | solution.py:88
  202.7 0.9 fusion.21
  203.6 0.1 reshape.110
  203.7 8.2 %reshape.109 = bf16[1056,4096]{1,0:T(8,128)(2,1)} reshape(bf16[16,66,4096]{2,1,0:T(8,128)(2,1)} %all-to-all-done) | data formatting | bytes 17301504 | tf_op jit(solution)/shard_map/reshape | solution.py:80
  211.9 13.0 %fusion.41 = f32[1056,1024]{1,0:T(8,128)S(1)} fusion(bf16[1056,4096]{1,0:T(8,128)(2,1)} %reshape.109, bf16[1024,4096]{1,0:T(8,128)(2,1)} %select_dynamic-update-slice_fusion), kind=kOutput, calls=%fused_computation.108 | convolution fusion | flops 8858370048 | bytes 21364736 | tf_op jit(solution)/shard_map/dot_general | solution.py:121
  224.9 1.4 fusion.37
  226.3 0.4 select_reduce_fusion.7
  226.7 0.4 fusion.13
  227.1 0.5 select_reduce_fusion.6
  227.6 0.5 fusion.12
  228.1 0.8 select_reduce_fusion.5
  228.9 0.7 fusion.36
  229.5 0.9 select_reduce_fusion.4
  230.5 0.8 fusion.11
  231.3 1.1 select_reduce_fusion.3
  232.4 1.0 fusion.20
  233.5 1.3 select_reduce_fusion.2
  234.7 1.2 fusion.10
  236.0 1.5 select_reduce_fusion.1
  237.4 1.4 select_reduce_fusion
  238.9 0.1 collective-permute-start.6
  239.0 0.1 collective-permute-start.7
  239.0 3.0 %collective-permute-start.8 = (f32[128,8]{0,1:T(8,128)S(1)}, f32[128,8]{0,1:T(8,128)S(1)}, u32[]{:S(2)}, u32[]{:S(2)}) collective-permute-start(f32[128,8]{0,1:T(8,128)S(1)} %get-tuple-element.18), channel_id=1, source_target_pairs={{2,1},{16,3},{18,17},{0,19},{19,0},{1,2},{3,16},{17,18},{6,5},{20,... | collective-permute-start | bytes 12296 | tf_op jit(solution)/shard_map/ppermute | solution.py:67
  242.0 0.6 collective-permute-done.7
  242.6 0.7 collective-permute-done.8
  243.4 0.1 copy.36
  243.5 0.7 gather_fusion
  244.2 0.1 broadcast_select_fusion
  244.3 0.7 copy.37
  (28 shorter events, 0.3 us)
Async XLA Ops:
  20.3 7.2 %copy-start.1 = (s32[256,1]{0,1:T(1,128)S(1)}, s32[256,1]{0,1:T(1,128)}, u32[]{:S(2)}) copy-start(s32[256,1]{0,1:T(1,128)} %param.7) | copy-start | bytes 3076
  20.3 8.9 %copy-start = (bf16[256,4096]{1,0:T(8,128)(2,1)S(1)}, bf16[256,4096]{1,0:T(8,128)(2,1)}, u32[]{:S(2)}) copy-start(bf16[256,4096]{1,0:T(8,128)(2,1)} %param.6) | copy-start | bytes 6291460
  20.3 169.2 %all-to-all-start = ((bf16[16,66,4096]{2,1,0:T(8,128)(2,1)}), bf16[16,66,4096]{2,1,0:T(8,128)(2,1)}, u32[]{:S(2)}, u32[]{:S(2)}) async-start(bf16[16,66,4096]{2,1,0:T(8,128)(2,1)} %stack.30), calls=%async_computation | async-start | bytes 18874368 | tf_op jit(solution)/shard_map/all_to_all | solution.py:81
  32.7 5.4 %copy-start.2 = (s32[256]{0:T(256)S(1)}, s32[256]{0:T(256)}, u32[]{:S(2)}) copy-start(s32[256]{0:T(256)} %param.8) | copy-start | bytes 3076
  32.7 5.4 %copy-start.3 = (s32[256]{0:T(256)S(1)}, s32[256]{0:T(256)}, u32[]{:S(2)}) copy-start(s32[256]{0:T(256)} %param.9) | copy-start | bytes 3076
  34.4 27.5 %collective-permute-start.3 = (bf16[128,4096]{1,0:T(8,128)(2,1)S(1)}, bf16[128,4096]{1,0:T(8,128)(2,1)S(1)}, u32[]{:S(2)}, u32[]{:S(2)}) collective-permute-start(bf16[128,4096]{1,0:T(8,128)(2,1)S(1)} %get-tuple-element.16), channel_id=1, source_target_pairs={{0,1},{1,0},{2,3},{3,2},{16,17},{17,16},{18,19},{19,18},{4,5},{5,4... | collective-permute-start | bytes 3145736 | tf_op jit(solution)/shard_map/ppermute | solution.py:67
  34.4 27.6 %collective-permute-start.4 = (bf16[128,4096]{1,0:T(8,128)(2,1)S(1)}, bf16[128,4096]{1,0:T(8,128)(2,1)S(1)}, u32[]{:S(2)}, u32[]{:S(2)}) collective-permute-start(bf16[128,4096]{1,0:T(8,128)(2,1)S(1)} %get-tuple-element.15), channel_id=1, source_target_pairs={{0,2},{2,16},{16,18},{18,0},{1,19},{3,1},{17,3},{19,17},{4,6},{6,2... | collective-permute-start | bytes 3145736 | tf_op jit(solution)/shard_map/ppermute | solution.py:67
  35.7 26.2 %collective-permute-start.5 = (bf16[128,4096]{1,0:T(8,128)(2,1)S(1)}, bf16[128,4096]{1,0:T(8,128)(2,1)S(1)}, u32[]{:S(2)}, u32[]{:S(2)}) collective-permute-start(bf16[128,4096]{1,0:T(8,128)(2,1)S(1)} %get-tuple-element.14), channel_id=1, source_target_pairs={{1,2},{3,16},{17,18},{19,0},{0,19},{2,1},{16,3},{18,17},{5,6},{7,2... | collective-permute-start | bytes 3145736 | tf_op jit(solution)/shard_map/ppermute | solution.py:67
  38.3 1.8 collective-permute-start
  38.4 23.1 %collective-permute-start.1 = (s32[2,128]{1,0:T(2,128)S(1)}, s32[2,128]{1,0:T(2,128)S(1)}, u32[]{:S(2)}, u32[]{:S(2)}) collective-permute-start(s32[2,128]{1,0:T(2,128)S(1)} %get-tuple-element.26), channel_id=1, source_target_pairs={{0,2},{2,16},{16,18},{18,0},{1,19},{3,1},{17,3},{19,17},{4,6},{6,2... | collective-permute-start | bytes 3080 | tf_op jit(solution)/shard_map/ppermute | solution.py:67
  40.1 21.8 %collective-permute-start.2 = (s32[2,128]{1,0:T(2,128)S(1)}, s32[2,128]{1,0:T(2,128)S(1)}, u32[]{:S(2)}, u32[]{:S(2)}) collective-permute-start(s32[2,128]{1,0:T(2,128)S(1)} %get-tuple-element.25), channel_id=1, source_target_pairs={{1,2},{3,16},{17,18},{19,0},{0,19},{2,1},{16,3},{18,17},{5,6},{7,2... | collective-permute-start | bytes 3080 | tf_op jit(solution)/shard_map/ppermute | solution.py:67
  238.9 3.2 %collective-permute-start.6 = (f32[128,8]{0,1:T(8,128)S(1)}, f32[128,8]{0,1:T(8,128)S(1)}, u32[]{:S(2)}, u32[]{:S(2)}) collective-permute-start(f32[128,8]{0,1:T(8,128)S(1)} %get-tuple-element.20), channel_id=1, source_target_pairs={{1,0},{0,1},{3,2},{2,3},{17,16},{16,17},{19,18},{18,19},{5,4},{4,5... | collective-permute-start | bytes 12296 | tf_op jit(solution)/shard_map/ppermute | solution.py:67
  239.0 3.7 %collective-permute-start.7 = (f32[128,8]{0,1:T(8,128)S(1)}, f32[128,8]{0,1:T(8,128)S(1)}, u32[]{:S(2)}, u32[]{:S(2)}) collective-permute-start(f32[128,8]{0,1:T(8,128)S(1)} %get-tuple-element.19), channel_id=1, source_target_pairs={{2,0},{16,2},{18,16},{0,18},{19,1},{1,3},{3,17},{17,19},{6,4},{20,... | collective-permute-start | bytes 12296 | tf_op jit(solution)/shard_map/ppermute | solution.py:67
  239.0 4.3 %collective-permute-start.8 = (f32[128,8]{0,1:T(8,128)S(1)}, f32[128,8]{0,1:T(8,128)S(1)}, u32[]{:S(2)}, u32[]{:S(2)}) collective-permute-start(f32[128,8]{0,1:T(8,128)S(1)} %get-tuple-element.18), channel_id=1, source_target_pairs={{2,1},{16,3},{18,17},{0,19},{19,0},{1,2},{3,16},{17,18},{6,5},{20,... | collective-permute-start | bytes 12296 | tf_op jit(solution)/shard_map/ppermute | solution.py:67
